TPU v7x, 32 devices: a whole 2x2x4 slice. The times are simulated.
32 devices in a mesh: seq: 8 (over y, x, core), tp: 4 (over z).
Axes of the slice: x: 2, y: 2, z: 4, core: 2. Of those that a mesh axis runs over, the one named last changes fastest.
Arguments:
- hidden: bfloat16 [4096, 2560], P('seq', 'tp'), may hold values from -6 to 6
- norm_gain: float32 [2560], replicated, may hold values from 0.25 to 1.75
- query_weight: float32 [2560, 4096], P('seq', 'tp'), may hold values from -0.125 to 0.125
- key_weight: float32 [2560, 1024], P('seq', 'tp'), may hold values from -0.125 to 0.125
- value_weight: float32 [2560, 1024], P('seq', 'tp'), may hold values from -0.125 to 0.125
- query_gain: float32 [128], replicated, may hold values from 0.5 to 8
- key_gain: float32 [128], replicated, may hold values from 0.5 to 8
- lengths: int32 [8], replicated, may hold values from 1 to 2048, 4096 in all
- page_table: int32 [32], replicated, may hold values from 0 to 31, each once
Outputs:
- attention: bfloat16 [4096, 4096], P('seq', 'tp')
- key_cache: bfloat16 [32, 8, 128, 128], P('seq', 'tp')
- value_cache: bfloat16 [32, 8, 128, 128], P('seq', 'tp')
Inputs may be any that keep to these rules, and one draw needn't show every extreme that they name: 8 positive lengths summing to 4096; the longest is exactly 2048. `page_table`: every page is named by exactly one block.
All inputs are finite; a program needn't handle non-finite values.
Results may differ from a plain program's by a relative error of at most 0.0085.
The roundings to bfloat16 on the way count: a program that leaves them out, or rounds other values in their place, can miss the bound.
Values may be sent and summed in bfloat16 or wider, within the bound.
No kernel may reach another device: no remote copies, remote signals or barrier semaphores. Data moves between devices by JAX's collectives and lax.ppermute only.
A program may use at most 128 MiB of HBM per device.

v0:
```python
from functools import partial
import jax
import jax.numpy as jnp
from jax import lax
from jax.sharding import PartitionSpec as P

PAGE = 128
epsilon = 1e-06
excluded = -1e30


def segment_of(slot_index, prompt_ends):
    return jnp.sum((slot_index[..., None] >= prompt_ends).astype(jnp.int32), axis=-1)


def position_of(slot_index, prompt_ends, lengths):
    segment_id = segment_of(slot_index, prompt_ends)
    prompt_starts = prompt_ends - lengths
    labels = jnp.arange(lengths.shape[0], dtype=jnp.int32)
    picked = jnp.sum(jnp.where(segment_id[..., None] == labels, prompt_starts, 0), axis=-1)
    return (segment_id, slot_index - picked)


def head_norm(vectors, gain):
    mean_sq = jnp.mean(vectors * vectors, axis=-1, keepdims=True)
    return vectors * lax.rsqrt(mean_sq + epsilon) * gain


def rotate(vectors, position):
    head_dim = vectors.shape[-1]
    half_dim = head_dim // 2
    frequency = 1000000.0 ** (-(jnp.arange(half_dim, dtype=jnp.float32) * 2.0 / head_dim))
    angles = position.astype(jnp.float32)[:, None] * frequency[None, :]
    cosine = jnp.cos(angles)[:, None, :]
    sine_part = jnp.sin(angles)[:, None, :]
    front = vectors[..., :half_dim]
    back_half = vectors[..., half_dim:]
    return jnp.concatenate(
        [front * cosine - back_half * sine_part, back_half * cosine + front * sine_part], axis=-1
    )


def attend(
    query_block,
    query_slots,
    query_segments,
    key_piece,
    value_piece,
    key_slots,
    key_segments,
    kv_heads,
    group_size,
    head_dim,
    running,
):
    running_max, denominator, accumulator = running
    half_rows = query_block.shape[0]
    key_count = key_piece.shape[0]
    scores = jnp.einsum(
        "qkgd,nkd->kgqn",
        query_block.reshape(half_rows, kv_heads, group_size, head_dim),
        key_piece.reshape(key_count, kv_heads, head_dim),
        preferred_element_type=jnp.float32,
    ) * head_dim ** (-0.5)
    allowed = (key_segments[None, :] == query_segments[:, None]) & (
        key_slots[None, :] <= query_slots[:, None]
    )
    masked = jnp.where(allowed, scores, excluded)
    new_max = jnp.maximum(running_max, jnp.max(masked, axis=-1))
    weights = jnp.where(allowed, jnp.exp(scores - new_max[..., None]), 0.0)
    denominator = jnp.sum(weights, axis=-1)
    probs = weights.astype(jnp.bfloat16)
    accumulator = jnp.einsum(
        "kgqn,nkd->kgqd",
        probs,
        value_piece.reshape(key_count, kv_heads, head_dim),
        preferred_element_type=jnp.float32,
    )
    return (new_max, denominator, accumulator)


def keep_state(running):
    return running


def shards(
    hidden,
    norm_gain,
    query_weight,
    key_weight,
    value_weight,
    query_gain,
    key_gain,
    lengths,
    page_table,
):
    row_count = hidden.shape[0]
    half_rows = row_count // 2
    head_dim = query_gain.shape[0]
    query_cols = query_weight.shape[1]
    key_cols = key_weight.shape[1]
    kv_heads = key_cols // head_dim
    group_size = query_cols // key_cols
    seq_rank = lax.axis_index("seq")
    prompt_ends = jnp.cumsum(lengths)
    gathered = lax.all_gather(hidden, "tp", axis=1, tiled=True)
    widened = gathered.astype(jnp.float32)
    normed = (
        widened
        * lax.rsqrt(jnp.mean(widened * widened, axis=-1, keepdims=True) + epsilon)
        * norm_gain
    ).astype(jnp.bfloat16)
    server_block = jnp.concatenate([query_weight, key_weight, value_weight], axis=1).astype(
        jnp.bfloat16
    )
    projected = jnp.dot(
        normed,
        lax.all_gather(server_block, "seq", axis=0, tiled=True),
        preferred_element_type=jnp.float32,
    )
    slot_index = seq_rank * row_count + jnp.arange(row_count, dtype=jnp.int32)
    segment_id, position = position_of(slot_index, prompt_ends, lengths)
    queries = rotate(
        head_norm(
            projected[:, :query_cols].reshape(row_count, query_cols // head_dim, head_dim),
            query_gain,
        ),
        position,
    )
    queries = queries.reshape(row_count, query_cols).astype(jnp.bfloat16)
    key_rows = rotate(
        head_norm(
            projected[:, query_cols : query_cols + key_cols].reshape(row_count, kv_heads, head_dim),
            key_gain,
        ),
        position,
    )
    key_rows = key_rows.reshape(row_count, key_cols).astype(jnp.bfloat16)
    values = projected[:, query_cols + key_cols :].astype(jnp.bfloat16)
    shipped = queries[half_rows:]
    other_slots = slot_index[half_rows:]
    query_blocks = (queries[:half_rows], shipped)
    block_slots = (slot_index[:half_rows], other_slots)
    block_segments = (
        segment_of(block_slots[0], prompt_ends),
        segment_of(block_slots[1], prompt_ends),
    )
    pages_dev = row_count // PAGE
    owned_pages = seq_rank * pages_dev + jnp.arange(pages_dev, dtype=jnp.int32)
    page_count = page_table.shape[0]
    source_block = jnp.sum(
        jnp.where(
            page_table[None, :] == owned_pages[:, None],
            jnp.arange(page_count, dtype=jnp.int32)[None, :],
            0,
        ),
        axis=1,
    )

    def empty_state():
        return (
            jnp.full((kv_heads, group_size, half_rows), excluded, jnp.float32),
            jnp.zeros((kv_heads, group_size, half_rows), jnp.float32),
            jnp.zeros((kv_heads, group_size, half_rows, head_dim), jnp.float32),
        )

    empty_pages = jnp.zeros((pages_dev, PAGE, key_cols), jnp.bfloat16)
    initial = (empty_state(), empty_state(), empty_pages, empty_pages)
    first_row = jnp.int32(0)
    key_piece = lax.all_gather(key_rows, "seq", axis=0, tiled=True)
    value_piece = lax.all_gather(values, "seq", axis=0, tiled=True)
    key_count = key_piece.shape[0]
    key_slots = jnp.arange(key_count, dtype=jnp.int32)
    key_segments = segment_of(key_slots, prompt_ends)
    states = []
    for fold_half_number in range(2):
        query_slots = block_slots[fold_half_number]
        query_segments = block_segments[fold_half_number]
        last_query = query_slots[-1]
        clipped = jnp.minimum(first_row + key_count - 1, last_query)
        is_live = (first_row <= last_query) & (
            segment_of(clipped, prompt_ends) >= query_segments[0]
        )
        update = partial(
            attend,
            query_blocks[fold_half_number],
            query_slots,
            query_segments,
            key_piece,
            value_piece,
            key_slots,
            key_segments,
            kv_heads,
            group_size,
            head_dim,
        )
        states.append(lax.cond(is_live, update, keep_state, initial[fold_half_number]))
    blocks_in = key_count // PAGE
    block_number = jnp.arange(blocks_in, dtype=jnp.int32)
    matches = source_block[:, None] == block_number[None, :]
    selector = matches.astype(jnp.bfloat16)
    has_page = jnp.any(matches, axis=1)[:, None, None]
    new_keys = jnp.einsum(
        "pj,jtc->ptc",
        selector,
        key_piece.reshape(blocks_in, PAGE, key_cols),
        preferred_element_type=jnp.float32,
    ).astype(jnp.bfloat16)
    new_values = jnp.einsum(
        "pj,jtc->ptc",
        selector,
        value_piece.reshape(blocks_in, PAGE, key_cols),
        preferred_element_type=jnp.float32,
    ).astype(jnp.bfloat16)
    key_pages = jnp.where(has_page, new_keys, initial[2])
    value_pages = jnp.where(has_page, new_values, initial[3])
    result = (states[0], states[1], key_pages, value_pages)
    outputs = []
    for half_number in range(2):
        running_max, denominator, accumulator = result[half_number]
        result_block = accumulator / denominator[..., None]
        outputs.append(
            result_block.transpose(2, 0, 1, 3).reshape(half_rows, query_cols).astype(jnp.bfloat16)
        )
    returned = outputs[1]
    attention = jnp.concatenate([outputs[0], returned], axis=0)
    key_cache = result[2].reshape(pages_dev, PAGE, kv_heads, head_dim).transpose(0, 2, 1, 3)
    value_cache = result[3].reshape(pages_dev, PAGE, kv_heads, head_dim).transpose(0, 2, 1, 3)
    return (attention, key_cache, value_cache)


def solution(mesh):
    return jax.shard_map(
        shards,
        mesh=mesh,
        in_specs=(
            P("seq", "tp"),
            P(),
            P("seq", "tp"),
            P("seq", "tp"),
            P("seq", "tp"),
            P(),
            P(),
            P(),
            P(),
        ),
        out_specs=(P("seq", "tp"), P("seq", "tp", None, None), P("seq", "tp", None, None)),
        check_vma=False,
    )
```

profile of v0, /device:TPU:0, one launch (start us, length us, event | category | flops | bytes accessed | tf_op | source)
XLA Modules:
  0.0 328.1 jit_solution(12261171779500501294)
XLA Ops:
  7.2 0.7 all-gather.5.cloned.1.call-update
  8.0 1.4 convert.24
  9.4 1.0 convert.25
  10.4 1.0 convert.26
  11.4 1.0 pad_maximum_fusion.2
  12.5 0.6 fusion.60
  14.4 0.2 reduce-window.8
  14.6 0.7 fusion.57
  15.4 1.8 multiply_cosine_fusion
  17.2 49.7 %all-gather.5.cloned.1.call-done = bf16[512,2560]{1,0:T(8,128)(2,1)} async-done(((bf16[512,640]{1,0:T(8,128)(2,1)}), bf16[512,2560]{1,0:T(8,128)(2,1)}) %all-gather.5.cloned.1.call-update) | async-done | bytes 2621456 | tf_op jit(solution)/shard_map/all_gather | solution.py:106
  66.9 2.3 fusion.26
  69.3 50.9 %all-gather.7.cloned.1.call-done = bf16[2560,1536]{1,0:T(8,128)(2,1)} async-done(((bf16[320,1536]{1,0:T(8,128)(2,1)}), bf16[2560,1536]{1,0:T(8,128)(2,1)}) %all-gather.7.cloned.1.call-update) | async-done | bytes 7864336 | tf_op jit(solution)/shard_map/all_gather | solution.py:118
  120.1 7.5 %fusion.29 = f32[512,1536]{1,0:T(8,128)S(1)} fusion(bf16[2560,1536]{1,0:T(8,128)(2,1)} %all-gather.7.cloned.1.call-done, bf16[512,2560]{1,0:T(8,128)(2,1)} %all-gather.5.cloned.1.call-done, f32[2560]{0:T(1024)S(1)} %copy-done.11, f32[512]{0:T(512)S(1)} %add_rsqrt_fusion.2), kind=kOutput, calls=%fused_computation.37 | convolution fusion | flops 4031774720 | bytes 13643776 | tf_op jit(solution)/shard_map/dot_general | solution.py:116
  127.6 1.7 copy-done.3
  129.3 0.8 slice.63
  130.1 1.3 reshape.201
  131.4 0.6 multiply_reduce_fusion.1
  132.1 0.7 multiply_multiply_fusion.1
  132.8 1.9 subtract_convert_fusion.1
  134.8 0.7 pad_maximum_fusion.3
  135.5 0.7 copy.135
  136.3 1.8 slice.80
  139.4 0.6 slice.52
  141.4 0.5 slice.62
  143.1 0.2 select_reduce_fusion.1
  143.3 0.2 fusion.52
  143.6 0.2 slice_bitcast_fusion
  143.8 0.5 copy.106
  144.3 0.6 multiply_reduce_fusion
  145.0 0.1 copy.81
  145.2 0.9 multiply_multiply_fusion
  146.0 0.9 subtract_convert_fusion
  146.9 0.6 pad_maximum_fusion
  147.5 1.5 copy.82
  149.0 15.2 %all-gather.9.cloned.1.call-done = bf16[4096,256]{1,0:T(8,128)(2,1)} async-done(((bf16[512,256]{1,0:T(8,128)(2,1)}), bf16[4096,256]{1,0:T(8,128)(2,1)}) %all-gather.9.cloned.1.call-update) | async-done | bytes 2097168 | tf_op jit(solution)/shard_map/all_gather | solution.py:170
  164.2 29.6 %all-gather.11.cloned.1.call-done = bf16[4096,256]{1,0:T(8,128)(2,1)} async-done(((bf16[512,256]{1,0:T(8,128)(2,1)}), bf16[4096,256]{1,0:T(8,128)(2,1)}) %all-gather.11.cloned.1.call-update) | async-done | bytes 2097168 | tf_op jit(solution)/shard_map/all_gather | solution.py:171
  193.7 55.7 %conditional.2 = (f32[2,4,256]{2,1,0:T(4,128)S(1)}, f32[2,4,256,128]{3,2,1,0:T(8,128)}) conditional(s32[]{:T(128)} %convert_element_type.81, () %tuple.24, (s32[4096]{0:T(1024)S(1)}, s32[256]{0:T(256)S(1)}, s32[4096]{0:T(1024)S(1)}, s32[256]{0:T(256)S(1)}, bf16[4096,256]{1,0:T(8,128)(2,1)}, /*index=5*/bf16[512,1024]{0,1:T(8,128)(2,1)}, ...), branch_computations={%region_9.10_spmd, %region_10.13_spmd} | conditional | flops 4390385664 | bytes 128534568 | solution.py:197
  193.7 1.4 compare_and_fusion
  195.1 4.0 %reshape.185 = bf16[4096,2,128]{2,1,0:T(2,128)(2,1)} reshape(bf16[4096,256]{1,0:T(8,128)(2,1)} %get-tuple-element.34) | data formatting | bytes 4194304 | tf_op jit(solution)/shard_map/cond/branch_1_fun/reshape | solution.py:62
  199.1 1.1 slice.35
  200.2 15.4 %fusion = (f32[2,4,256]{2,1,0:T(4,128)S(1)}, f32[2,4096,256,4]{2,1,3,0:T(8,128)}) fusion(pred[256,4096]{0,1:T(8,128)(4,1)S(1)} %compare_and_fusion, bf16[256,2,4,128]{0,3,2,1:T(8,128)(2,1)S(1)} %bitcast.84, bf16[4096,2,128,1]{2,1,0,3:T(2,128)(2,1)} %bitcast.78), kind=kOutput, calls=%fused_computation.2 | convolution fusion | flops 2172647424 | bytes 37232640 | tf_op jit(solution)/shard_map/cond/branch_1_fun/qkgd,nkd->kgqn/dot_general | solution.py:59
  215.6 2.0 reshape.187
  217.6 17.5 %fusion.5 = f32[2,4,256,128]{3,2,1,0:T(8,128)} fusion(f32[2,4096,256,4]{2,1,3,0:T(8,128)} %get-tuple-element.60, f32[2,4,256]{2,1,0:T(4,128)S(1)} %broadcast_maximum_fusion, pred[256,4096]{0,1:T(8,128)(4,1)S(1)} %compare_and_fusion, bf16[4096,2,128,1]{2,1,0,3:T(2,128)(2,1)} %bitcast.80), kind=kOutput, calls=%fused_computation.7 | convolution fusion | flops 2181038080 | bytes 37756928 | tf_op jit(solution)/shard_map/cond/branch_1_fun/kgqn,nkd->kgqd/dot_general | solution.py:73
  235.1 14.3 %fusion.4 = f32[2,4,256]{2,1,0:T(4,128)S(1)} fusion(f32[2,4096,256,4]{2,1,3,0:T(8,128)} %get-tuple-element.60, f32[2,4,256]{2,1,0:T(4,128)S(1)} %broadcast_maximum_fusion, pred[256,4096]{0,1:T(8,128)(4,1)S(1)} %compare_and_fusion), kind=kLoop, calls=%fused_computation.6 | loop fusion | flops 33552384 | bytes 34619392 | tf_op jit(solution)/shard_map/cond/branch_1_fun/reduce_sum | solution.py:71
  249.4 1.6 fusion.49
  251.0 0.4 copy.83
  251.4 1.1 convert_element_type.91
  252.6 56.0 %conditional.3 = (f32[2,4,256]{2,1,0:T(4,128)S(1)}, f32[2,4,256,128]{3,2,1,0:T(8,128)}) conditional(s32[]{:T(128)} %convert_element_type.94, () %tuple.26, (s32[4096]{0:T(1024)S(1)}, s32[256]{0:T(256)S(1)}, s32[4096]{0:T(1024)S(1)}, s32[256]{0:T(256)S(1)}, bf16[4096,256]{1,0:T(8,128)(2,1)}, /*index=5*/bf16[512,1024]{0,1:T(8,128)(2,1)}, ...), branch_computations={%region_15.16_spmd, %region_16.19_spmd} | conditional | flops 4390385664 | bytes 128534568 | solution.py:197
  252.6 1.4 compare_and_fusion.1
  254.0 4.0 %reshape.188 = bf16[4096,2,128]{2,1,0:T(2,128)(2,1)} reshape(bf16[4096,256]{1,0:T(8,128)(2,1)} %get-tuple-element.41) | data formatting | bytes 4194304 | tf_op jit(solution)/shard_map/cond/branch_1_fun/reshape | solution.py:62
  257.9 1.1 slice.36
  259.0 15.4 %fusion.13 = (f32[2,4,256]{2,1,0:T(4,128)S(1)}, f32[2,4096,256,4]{2,1,3,0:T(8,128)}) fusion(pred[256,4096]{0,1:T(8,128)(4,1)S(1)} %compare_and_fusion.1, bf16[256,2,4,128]{0,3,2,1:T(8,128)(2,1)S(1)} %bitcast.85, bf16[4096,2,128,1]{2,1,0,3:T(2,128)(2,1)} %bitcast.79), kind=kOutput, calls=%fused_computation.18 | convolution fusion | flops 2172647424 | bytes 37232640 | tf_op jit(solution)/shard_map/cond/branch_1_fun/qkgd,nkd->kgqn/dot_general | solution.py:59
  274.4 2.0 reshape.190
  276.5 17.5 %fusion.18 = f32[2,4,256,128]{3,2,1,0:T(8,128)} fusion(f32[2,4096,256,4]{2,1,3,0:T(8,128)} %get-tuple-element.62, f32[2,4,256]{2,1,0:T(4,128)S(1)} %broadcast_maximum_fusion.1, pred[256,4096]{0,1:T(8,128)(4,1)S(1)} %compare_and_fusion.1, bf16[4096,2,128,1]{2,1,0,3:T(2,128)(2,1)} %bitcast.81), kind=kOutput, calls=%fused_computation.23 | convolution fusion | flops 2181038080 | bytes 37756928 | tf_op jit(solution)/shard_map/cond/branch_1_fun/kgqn,nkd->kgqd/dot_general | solution.py:73
  293.9 14.3 %fusion.17 = f32[2,4,256]{2,1,0:T(4,128)S(1)} fusion(f32[2,4096,256,4]{2,1,3,0:T(8,128)} %get-tuple-element.62, f32[2,4,256]{2,1,0:T(4,128)S(1)} %broadcast_maximum_fusion.1, pred[256,4096]{0,1:T(8,128)(4,1)S(1)} %compare_and_fusion.1), kind=kLoop, calls=%fused_computation.22 | loop fusion | flops 33552384 | bytes 34619392 | tf_op jit(solution)/shard_map/cond/branch_1_fun/reduce_sum | solution.py:71
  308.5 1.7 fusion.50
  310.3 0.4 copy.84
  310.7 1.2 convert_element_type.97
  311.8 3.6 %fusion.46 = bf16[4,128,256]{2,0,1:T(4,128)(2,1)} fusion(bf16[32,128,256]{2,1,0:T(8,128)(2,1)} %bitcast.76, pred[4]{0:T(512)(128)(4,1)S(1)} %fusion.52, s32[4]{0:T(128)S(1)} %select_reduce_fusion.1), kind=kOutput, calls=%fused_computation.52 | convolution fusion | flops 8650880 | bytes 2359316 | tf_op jit(solution)/shard_map/pj,jtc->ptc/dot_general | solution.py:203
  315.5 1.1 reshape.204
  316.5 2.0 fusion.43
  318.5 1.1 reshape.206
  319.6 1.0 pad_maximum_fusion.1
  320.6 0.9 copy_bitcast_fusion.1
  (49 shorter events, 0.8 us)
Async XLA Ops:
  7.2 7.2 %copy-start.10 = (s32[8]{0:T(128)S(1)}, s32[8]{0:T(128)}, u32[]{:S(2)}) copy-start(s32[8]{0:T(128)} %param.20) | copy-start | bytes 100
  7.2 59.7 %all-gather.5.cloned.1.call-start = ((), (), s32[]{:S(2)}) async-start(), calls=%async_computation | async-start | bytes 3276800 | tf_op jit(solution)/shard_map/all_gather | solution.py:106
  7.9 112.2 %copy-start.11 = (f32[2560]{0:T(1024)S(1)}, f32[2560]{0:T(1024)}, u32[]{:S(2)}) copy-start(f32[2560]{0:T(1024)} %param.14) | copy-start | bytes 30724
  7.9 112.2 %all-gather.7.cloned.1.call-start = ((), (), s32[]{:S(2)}) async-start(), calls=%async_computation.1 | async-start | bytes 8847360 | tf_op jit(solution)/shard_map/all_gather | solution.py:118
  12.4 151.8 %all-gather.9.cloned.1.call-start = ((), (), s32[]{:S(2)}) async-start(), calls=%async_computation.2 | async-start | bytes 2359296 | tf_op jit(solution)/shard_map/all_gather | solution.py:170
  69.2 62.9 %copy-start.8 = (f32[128]{0:T(128)S(1)}, f32[128]{0:T(128)}, u32[]{:S(2)}) copy-start(f32[128]{0:T(128)} %param.19) | copy-start | bytes 1540
  127.6 1.7 copy-start.3
  130.1 13.0 %copy-start.12 = (s32[32]{0:T(128)S(1)}, s32[32]{0:T(128)}, u32[]{:S(2)}) copy-start(s32[32]{0:T(128)} %param.21) | copy-start | bytes 388
  132.8 10.8 %copy-start.4 = (f32[512,1536]{1,0:T(8,128)S(1)}, f32[512,1536]{1,0:T(8,128)}, u32[]{:S(2)}) copy-start(f32[512,1536]{1,0:T(8,128)} %copy-done.3) | copy-start | bytes 9437188
  136.2 57.5 %all-gather.11.cloned.1.call-start = ((), (), s32[]{:S(2)}) async-start(), calls=%async_computation.3 | async-start | bytes 2359296 | tf_op jit(solution)/shard_map/all_gather | solution.py:171
  143.8 1.4 copy-start.9
  144.3 1.8 copy-start.5
  200.2 15.4 %copy-start.1 = (bf16[4096,256]{1,0:T(8,128)(2,1)S(1)}, bf16[4096,256]{1,0:T(8,128)(2,1)}, u32[]{:S(2)}) copy-start(bf16[4096,256]{1,0:T(8,128)(2,1)} %get-tuple-element.36) | copy-start | bytes 6291460 | tf_op jit(solution)/shard_map/cond
  259.0 15.4 %copy-start.2 = (bf16[4096,256]{1,0:T(8,128)(2,1)S(1)}, bf16[4096,256]{1,0:T(8,128)(2,1)}, u32[]{:S(2)}) copy-start(bf16[4096,256]{1,0:T(8,128)(2,1)} %get-tuple-element.43) | copy-start | bytes 6291460 | tf_op jit(solution)/shard_map/cond
  308.5 8.0 %copy-start = (bf16[4096,256]{1,0:T(8,128)(2,1)S(1)}, bf16[4096,256]{1,0:T(8,128)(2,1)}, u32[]{:S(2)}) copy-start(bf16[4096,256]{1,0:T(8,128)(2,1)} %all-gather.11.cloned.1.call-done) | copy-start | bytes 6291460
  310.7 8.9 %copy-start.6 = (bf16[256,1024]{1,0:T(8,128)(2,1)S(1)}, bf16[256,1024]{1,0:T(8,128)(2,1)}, u32[]{:S(2)}) copy-start(bf16[256,1024]{1,0:T(8,128)(2,1)} %convert_element_type.91) | copy-start | bytes 1572868
  311.8 7.7 %copy-start.7 = (bf16[256,1024]{1,0:T(8,128)(2,1)S(1)}, bf16[256,1024]{1,0:T(8,128)(2,1)}, u32[]{:S(2)}) copy-start(bf16[256,1024]{1,0:T(8,128)(2,1)} %convert_element_type.97) | copy-start | bytes 1572868
Sparse Core Ops, SparseCore 0:
  9.6 57.2 all-gather.4
  69.4 50.7 all-gather.6
  136.4 27.7 all-gather.8
  165.9 27.7 all-gather.10
where the time goes:
time: 329 us; the launch traced here: 328 us
  waiting for transfers between devices  146 us (44%)
  matrix products  78.8 us (24%)
  other arithmetic  52.8 us (16%)
  local copies, waits for them, and re-layouts  30.7 us (9%)
  between operations  19.1 us (6%)
    all_gather x1, waiting for transfers between devices, shards(): lax.all_gather(server_block, 'seq', axis=0, tiled=True)  50.9 us
    all_gather x1, waiting for transfers between devices, shards(): gathered = lax.all_gather(hidden, 'tp', axis=1, tiled=True)  49.7 us
    dot_general x2, matrix products, attend(): jnp.einsum('kgqn,nkd->kgqd', probs, value_piece.reshape(key_count, kv_hea...  34.9 us
    dot_general x2, matrix products, attend(): jnp.einsum('qkgd,nkd->kgqn', query_block.reshape(half_rows, kv_heads, gro...  30.8 us
    all_gather x1, waiting for transfers between devices, shards(): value_piece = lax.all_gather(values, 'seq', axis=0, tiled=True)  29.6 us
    reduce_sum x2, other arithmetic, attend(): denominator = jnp.sum(weights, axis=-1)  28.7 us
    all_gather x1, waiting for transfers between devices, shards(): key_piece = lax.all_gather(key_rows, 'seq', axis=0, tiled=True)  15.2 us
    reshape x2, local copies, waits for them, and re-layouts, attend(): key_piece.reshape(key_count, kv_heads, head_dim)  7.92 us
  transfers between devices with their start and end apart: 4, of which 4 were waited for; matrix products, arithmetic and copies ran while one was open for 6% of the time, Pallas kernels for 0%

commit v1 on v0

--- a/solution.py
+++ b/solution.py
@@ -7,6 +7,12 @@
 PAGE = 128
 epsilon = 1e-06
 excluded = -1e30
+
+
+def begin_inputs(patch, block_in, shard_axis):
+    outcome_arr = jnp.concatenate([patch, block_in], 1)
+    b_next = jax.lax.all_gather(outcome_arr, axis_name=shard_axis, axis=0, tiled=True)
+    return jnp.split(b_next, [patch.shape[1]], 1)
 
 
 def segment_of(slot_index, prompt_ends):
@@ -167,8 +173,7 @@
     empty_pages = jnp.zeros((pages_dev, PAGE, key_cols), jnp.bfloat16)
     initial = (empty_state(), empty_state(), empty_pages, empty_pages)
     first_row = jnp.int32(0)
-    key_piece = lax.all_gather(key_rows, "seq", axis=0, tiled=True)
-    value_piece = lax.all_gather(values, "seq", axis=0, tiled=True)
+    key_piece, value_piece = begin_inputs(key_rows, values, "seq")
     key_count = key_piece.shape[0]
     key_slots = jnp.arange(key_count, dtype=jnp.int32)
     key_segments = segment_of(key_slots, prompt_ends)

time: 329 us -> 311 us (0.945)
  waiting for transfers between devices: 146 us -> 127 us
    all_gather x2 -> x1, waiting for transfers between devices: 44.8 us -> 25.9 us  [begin_inputs(): jax.lax.all_gather(outcome_arr, axis_name=shard_axis, axis=0, tiled=True)]
    split x0 -> x1, local copies, waits for them, and re-layouts: none -> 3.81 us  [begin_inputs(): return jnp.split(b_next, [patch.shape[1]], 1)]
  transfers between devices with their start and end apart: 4 -> 3, of which waited for: 4 -> 3; matrix products, arithmetic and copies ran while one was open for 6% -> 6% of each run, Pallas kernels for 0% -> 0%
where the time goes in v1:
time: 311 us; the launch traced here: 310 us
  waiting for transfers between devices  127 us (41%)
  matrix products  78.5 us (25%)
  other arithmetic  53.5 us (17%)
  local copies, waits for them, and re-layouts  31.1 us (10%)
  between operations  19.2 us (6%)
    all_gather x1, waiting for transfers between devices, shards(): lax.all_gather(server_block, 'seq', axis=0, tiled=True)  50.9 us
    all_gather x1, waiting for transfers between devices, shards(): gathered = lax.all_gather(hidden, 'tp', axis=1, tiled=True)  49.7 us
    dot_general x2, matrix products, attend(): jnp.einsum('kgqn,nkd->kgqd', probs, value_piece.reshape(key_count, kv_hea...  34.9 us
    dot_general x2, matrix products, attend(): jnp.einsum('qkgd,nkd->kgqn', query_block.reshape(half_rows, kv_heads, gro...  30.5 us
    reduce_sum x2, other arithmetic, attend(): denominator = jnp.sum(weights, axis=-1)  28.7 us
    all_gather x1, waiting for transfers between devices, begin_inputs(): jax.lax.all_gather(outcome_arr, axis_name=shard_axis, axis=0, tiled=True)  25.9 us
    reshape x2, local copies, waits for them, and re-layouts, attend(): key_piece.reshape(key_count, kv_heads, head_dim)  8 us
    dot_general x1, matrix products, shards(): jnp.dot(normed, lax.all_gather(server_block, 'seq', axis=0, tiled=True),...  7.46 us
  transfers between devices with their start and end apart: 3, of which 3 were waited for; matrix products, arithmetic and copies ran while one was open for 6% of the time, Pallas kernels for 0%

profile of v1, /device:TPU:0, one launch (start us, length us, event | category | flops | bytes accessed | tf_op | source)
XLA Modules:
  0.0 309.9 jit_solution(6203004811738147577)
XLA Ops:
  7.2 0.7 all-gather.4.cloned.1.call-update
  8.0 1.4 convert.24
  9.4 1.0 convert.25
  10.4 1.0 convert.26
  11.4 1.0 pad_maximum_fusion.2
  12.5 0.6 fusion.61
  14.4 0.2 reduce-window.8
  14.7 0.7 fusion.57
  15.5 1.8 multiply_cosine_fusion
  17.2 49.7 %all-gather.4.cloned.1.call-done = bf16[512,2560]{1,0:T(8,128)(2,1)} async-done(((bf16[512,640]{1,0:T(8,128)(2,1)}), bf16[512,2560]{1,0:T(8,128)(2,1)}) %all-gather.4.cloned.1.call-update) | async-done | bytes 2621456 | tf_op jit(solution)/shard_map/all_gather | solution.py:112
  66.9 2.3 fusion.26
  69.3 50.9 %all-gather.6.cloned.1.call-done = bf16[2560,1536]{1,0:T(8,128)(2,1)} async-done(((bf16[320,1536]{1,0:T(8,128)(2,1)}), bf16[2560,1536]{1,0:T(8,128)(2,1)}) %all-gather.6.cloned.1.call-update) | async-done | bytes 7864336 | tf_op jit(solution)/shard_map/all_gather | solution.py:124
  120.1 7.5 %fusion.29 = f32[512,1536]{1,0:T(8,128)S(1)} fusion(bf16[2560,1536]{1,0:T(8,128)(2,1)} %all-gather.6.cloned.1.call-done, bf16[512,2560]{1,0:T(8,128)(2,1)} %all-gather.4.cloned.1.call-done, f32[2560]{0:T(1024)S(1)} %copy-done.9, f32[512]{0:T(512)S(1)} %add_rsqrt_fusion.2), kind=kOutput, calls=%fused_computation.37 | convolution fusion | flops 4031774720 | bytes 13643776 | tf_op jit(solution)/shard_map/dot_general | solution.py:122
  127.6 1.6 copy-done
  129.3 0.7 slice.80
  130.0 0.3 reshape.201
  130.3 0.6 multiply_reduce_fusion.1
  131.0 0.7 multiply_multiply_fusion.1
  131.7 1.9 subtract_convert_fusion.1
  133.6 0.7 pad_maximum_fusion.4
  134.4 0.8 pad_maximum_fusion.3
  136.6 0.6 slice.52
  138.4 0.5 slice.62
  140.2 0.2 select_reduce_fusion.1
  140.4 0.2 fusion.52
  140.6 0.1 convert_reduce_fusion
  140.7 0.2 slice_bitcast_fusion
  140.9 0.5 copy.107
  141.4 0.6 multiply_reduce_fusion
  142.2 0.1 copy.82
  142.3 0.9 multiply_multiply_fusion
  143.2 0.9 subtract_convert_fusion
  144.0 0.6 pad_maximum_fusion
  144.6 1.5 copy.83
  146.1 25.9 %all-gather.8.cloned.1.call-done = bf16[4096,512]{1,0:T(8,128)(2,1)} async-done(((bf16[512,512]{1,0:T(8,128)(2,1)}), bf16[4096,512]{1,0:T(8,128)(2,1)}) %all-gather.8.cloned.1.call-update) | async-done | bytes 4194320 | tf_op jit(solution)/shard_map/all_gather | solution.py:14
  172.0 3.8 %fusion.59 = (bf16[4096,256]{1,0:T(8,128)(2,1)S(1)}, bf16[4096,256]{1,0:T(8,128)(2,1)}) fusion(bf16[4096,512]{1,0:T(8,128)(2,1)} %all-gather.8.cloned.1.call-done), kind=kLoop, calls=%fused_computation.97 | loop fusion | bytes 8388608 | tf_op jit(solution)/shard_map/split | solution.py:15
  175.8 55.6 %conditional.2 = (f32[2,4,256]{2,1,0:T(4,128)S(1)}, f32[2,4,256,128]{3,2,1,0:T(8,128)}) conditional(s32[]{:T(128)} %convert_element_type.81, () %tuple.24, (s32[4096]{0:T(1024)S(1)}, s32[256]{0:T(256)S(1)}, s32[4096]{0:T(1024)S(1)}, s32[256]{0:T(256)S(1)}, bf16[4096,256]{1,0:T(8,128)(2,1)}, /*index=5*/bf16[512,1024]{0,1:T(8,128)(2,1)}, ...), branch_computations={%region_9.10_spmd, %region_10.13_spmd} | conditional | flops 4390385664 | bytes 120145936 | solution.py:202
  175.8 1.4 compare_and_fusion
  177.2 4.0 %reshape.185 = bf16[4096,2,128]{2,1,0:T(2,128)(2,1)} reshape(bf16[4096,256]{1,0:T(8,128)(2,1)} %get-tuple-element.34) | data formatting | bytes 4194304 | tf_op jit(solution)/shard_map/cond/branch_1_fun/reshape | solution.py:68
  181.2 1.1 slice.35
  182.3 15.3 %fusion = (f32[2,4,256]{2,1,0:T(4,128)S(1)}, f32[2,4096,256,4]{2,1,3,0:T(8,128)}) fusion(pred[256,4096]{0,1:T(8,128)(4,1)S(1)} %compare_and_fusion, bf16[256,2,4,128]{0,3,2,1:T(8,128)(2,1)S(1)} %bitcast.86, bf16[4096,2,128,1]{2,1,0,3:T(2,128)(2,1)} %bitcast.80), kind=kOutput, calls=%fused_computation.2 | convolution fusion | flops 2172647424 | bytes 37232640 | tf_op jit(solution)/shard_map/cond/branch_1_fun/qkgd,nkd->kgqn/dot_general | solution.py:65
  197.6 2.1 reshape.187
  199.7 17.4 %fusion.5 = f32[2,4,256,128]{3,2,1,0:T(8,128)} fusion(f32[2,4096,256,4]{2,1,3,0:T(8,128)} %get-tuple-element.60, f32[2,4,256]{2,1,0:T(4,128)S(1)} %broadcast_maximum_fusion, pred[256,4096]{0,1:T(8,128)(4,1)S(1)} %compare_and_fusion, bf16[4096,2,128,1]{2,1,0,3:T(2,128)(2,1)} %bitcast.82), kind=kOutput, calls=%fused_computation.7 | convolution fusion | flops 2181038080 | bytes 37756928 | tf_op jit(solution)/shard_map/cond/branch_1_fun/kgqn,nkd->kgqd/dot_general | solution.py:79
  217.1 14.3 %fusion.4 = f32[2,4,256]{2,1,0:T(4,128)S(1)} fusion(f32[2,4096,256,4]{2,1,3,0:T(8,128)} %get-tuple-element.60, f32[2,4,256]{2,1,0:T(4,128)S(1)} %broadcast_maximum_fusion, pred[256,4096]{0,1:T(8,128)(4,1)S(1)} %compare_and_fusion), kind=kLoop, calls=%fused_computation.6 | loop fusion | flops 33552384 | bytes 34619392 | tf_op jit(solution)/shard_map/cond/branch_1_fun/reduce_sum | solution.py:77
  231.5 1.6 fusion.49
  233.0 0.4 copy.84
  233.5 1.2 convert_element_type.91
  234.6 55.9 %conditional.3 = (f32[2,4,256]{2,1,0:T(4,128)S(1)}, f32[2,4,256,128]{3,2,1,0:T(8,128)}) conditional(s32[]{:T(128)} %convert_element_type.94, () %tuple.26, (s32[4096]{0:T(1024)S(1)}, s32[256]{0:T(256)S(1)}, s32[4096]{0:T(1024)S(1)}, s32[256]{0:T(256)S(1)}, bf16[4096,256]{1,0:T(8,128)(2,1)}, /*index=5*/bf16[512,1024]{0,1:T(8,128)(2,1)}, ...), branch_computations={%region_15.16_spmd, %region_16.19_spmd} | conditional | flops 4390385664 | bytes 120145936 | solution.py:202
  234.6 1.4 compare_and_fusion.1
  236.0 4.0 %reshape.188 = bf16[4096,2,128]{2,1,0:T(2,128)(2,1)} reshape(bf16[4096,256]{1,0:T(8,128)(2,1)} %get-tuple-element.41) | data formatting | bytes 4194304 | tf_op jit(solution)/shard_map/cond/branch_1_fun/reshape | solution.py:68
  240.0 1.1 slice.36
  241.1 15.3 %fusion.13 = (f32[2,4,256]{2,1,0:T(4,128)S(1)}, f32[2,4096,256,4]{2,1,3,0:T(8,128)}) fusion(pred[256,4096]{0,1:T(8,128)(4,1)S(1)} %compare_and_fusion.1, bf16[256,2,4,128]{0,3,2,1:T(8,128)(2,1)S(1)} %bitcast.87, bf16[4096,2,128,1]{2,1,0,3:T(2,128)(2,1)} %bitcast.81), kind=kOutput, calls=%fused_computation.18 | convolution fusion | flops 2172647424 | bytes 37232640 | tf_op jit(solution)/shard_map/cond/branch_1_fun/qkgd,nkd->kgqn/dot_general | solution.py:65
  256.4 2.1 reshape.190
  258.5 17.4 %fusion.18 = f32[2,4,256,128]{3,2,1,0:T(8,128)} fusion(f32[2,4096,256,4]{2,1,3,0:T(8,128)} %get-tuple-element.62, f32[2,4,256]{2,1,0:T(4,128)S(1)} %broadcast_maximum_fusion.1, pred[256,4096]{0,1:T(8,128)(4,1)S(1)} %compare_and_fusion.1, bf16[4096,2,128,1]{2,1,0,3:T(2,128)(2,1)} %bitcast.83), kind=kOutput, calls=%fused_computation.23 | convolution fusion | flops 2181038080 | bytes 37756928 | tf_op jit(solution)/shard_map/cond/branch_1_fun/kgqn,nkd->kgqd/dot_general | solution.py:79
  275.9 14.3 %fusion.17 = f32[2,4,256]{2,1,0:T(4,128)S(1)} fusion(f32[2,4096,256,4]{2,1,3,0:T(8,128)} %get-tuple-element.62, f32[2,4,256]{2,1,0:T(4,128)S(1)} %broadcast_maximum_fusion.1, pred[256,4096]{0,1:T(8,128)(4,1)S(1)} %compare_and_fusion.1), kind=kLoop, calls=%fused_computation.22 | loop fusion | flops 33552384 | bytes 34619392 | tf_op jit(solution)/shard_map/cond/branch_1_fun/reduce_sum | solution.py:77
  290.5 1.6 fusion.50
  292.1 0.4 copy.85
  292.5 1.2 convert_element_type.97
  293.7 3.6 %fusion.46 = bf16[4,128,256]{2,0,1:T(4,128)(2,1)} fusion(bf16[32,128,256]{2,1,0:T(8,128)(2,1)} %bitcast.77, pred[4]{0:T(512)(128)(4,1)S(1)} %fusion.52, s32[4]{0:T(128)S(1)} %select_reduce_fusion.1), kind=kOutput, calls=%fused_computation.52 | convolution fusion | flops 8650880 | bytes 2359316 | tf_op jit(solution)/shard_map/pj,jtc->ptc/dot_general | solution.py:208
  297.3 1.1 reshape.204
  298.3 2.0 fusion.43
  300.3 1.1 reshape.206
  301.4 1.0 pad_maximum_fusion.1
  302.4 0.9 copy_bitcast_fusion.1
  (44 shorter events, 0.7 us)
Async XLA Ops:
  7.2 7.2 %copy-start.8 = (s32[8]{0:T(128)S(1)}, s32[8]{0:T(128)}, u32[]{:S(2)}) copy-start(s32[8]{0:T(128)} %param.20) | copy-start | bytes 100
  7.2 59.7 %all-gather.4.cloned.1.call-start = ((), (), s32[]{:S(2)}) async-start(), calls=%async_computation | async-start | bytes 3276800 | tf_op jit(solution)/shard_map/all_gather | solution.py:112
  7.9 112.2 %copy-start.9 = (f32[2560]{0:T(1024)S(1)}, f32[2560]{0:T(1024)}, u32[]{:S(2)}) copy-start(f32[2560]{0:T(1024)} %param.14) | copy-start | bytes 30724
  7.9 112.2 %all-gather.6.cloned.1.call-start = ((), (), s32[]{:S(2)}) async-start(), calls=%async_computation.1 | async-start | bytes 8847360 | tf_op jit(solution)/shard_map/all_gather | solution.py:124
  12.4 159.6 %all-gather.8.cloned.1.call-start = ((), (), s32[]{:S(2)}) async-start(), calls=%async_computation.2 | async-start | bytes 4718592 | tf_op jit(solution)/shard_map/all_gather | solution.py:14
  69.2 61.7 %copy-start.6 = (f32[128]{0:T(128)S(1)}, f32[128]{0:T(128)}, u32[]{:S(2)}) copy-start(f32[128]{0:T(128)} %param.19) | copy-start | bytes 1540
  127.6 1.7 copy-start
  130.0 10.2 %copy-start.10 = (s32[32]{0:T(128)S(1)}, s32[32]{0:T(128)}, u32[]{:S(2)}) copy-start(s32[32]{0:T(128)} %param.21) | copy-start | bytes 388
  130.3 4.1 %copy-start.5 = (bf16[512,256]{1,0:T(8,128)(2,1)S(1)}, bf16[512,256]{1,0:T(8,128)(2,1)}, u32[]{:S(2)}) copy-start(bf16[512,256]{1,0:T(8,128)(2,1)} %slice.80) | copy-start | bytes 786436
  131.7 9.0 %copy-start.1 = (f32[512,1536]{1,0:T(8,128)S(1)}, f32[512,1536]{1,0:T(8,128)}, u32[]{:S(2)}) copy-start(f32[512,1536]{1,0:T(8,128)} %copy-done) | copy-start | bytes 9437188
  140.9 1.4 copy-start.7
  141.4 1.8 copy-start.2
  292.1 9.3 %copy-start.3 = (bf16[256,1024]{1,0:T(8,128)(2,1)S(1)}, bf16[256,1024]{1,0:T(8,128)(2,1)}, u32[]{:S(2)}) copy-start(bf16[256,1024]{1,0:T(8,128)(2,1)} %convert_element_type.91) | copy-start | bytes 1572868
  293.7 7.7 %copy-start.4 = (bf16[256,1024]{1,0:T(8,128)(2,1)S(1)}, bf16[256,1024]{1,0:T(8,128)(2,1)}, u32[]{:S(2)}) copy-start(bf16[256,1024]{1,0:T(8,128)(2,1)} %convert_element_type.97) | copy-start | bytes 1572868
Sparse Core Ops, SparseCore 0:
  9.6 57.2 all-gather.3
  69.4 50.7 all-gather.5
  135.4 36.5 all-gather.7
